TPU v7x, 128 devices: a whole 4x4x4 slice. The times are simulated.
128 devices in a mesh: row: 8 (over z, core), col: 16 (over x, y).
Axes of the slice: x: 4, y: 4, z: 4, core: 2. Of those that a mesh axis runs over, the one named last changes fastest.
Arguments:
- snapshots: float32 [512, 196608], P(('row', 'col')), may hold values from -6 to 6
- panels: float32 [8, 6, 32768, 256], P(None, None, ('row', 'col')), may hold values from -0.1875 to 0.1875
- diag_inverse: float32 [8, 256, 256], replicated, may hold values from -0.6 to 1.5, as said below
Outputs:
- whitened: float32 [6, 32768, 512], P(None, ('row', 'col'))
Inputs may be any that keep to these rules, and one draw needn't show every extreme that they name: Each block of diag_inverse is lower triangular with a diagonal of 0.5 to 1.5.
All inputs are finite; a program needn't handle non-finite values.
Results may differ from a plain program's by a relative error of at most 0.0001.
Values sent between devices are 32-bit elements; how exact they have to be, the bound alone decides.
No kernel may reach another device: no remote copies, remote signals or barrier semaphores. Data moves between devices by JAX's collectives and lax.ppermute only.
A program may use at most 128 MiB of HBM per device.

v0:
```python
import jax
import jax.numpy as jnp
from jax import lax
from jax.sharding import PartitionSpec as P


def spread(block, axis, owner):
    block = jnp.where(lax.axis_index(axis) == owner, block, jnp.zeros_like(block))
    return lax.psum(block, axis)


def per_device(snapshots, panels, diag_inverse):
    local_count, order_size = snapshots.shape
    sections, blocks, width_block, _ = panels.shape
    devices = lax.axis_size(("row", "col"))
    pieces = snapshots.reshape(local_count, blocks, devices, width_block)
    arrived = lax.all_to_all(pieces, ("row", "col"), split_axis=2, concat_axis=0, tiled=True)
    remaining = jnp.transpose(
        arrived.reshape(devices * local_count, blocks, width_block), (1, 2, 0)
    )
    device = lax.axis_index(("row", "col"))
    block_owner = lax.broadcasted_iota(jnp.int32, (blocks, 1, 1), 0) * devices + device
    for section in range(sections):
        solved = jnp.dot(
            diag_inverse[section],
            remaining[0],
            precision=lax.Precision.HIGHEST,
            preferred_element_type=jnp.float32,
        )
        solved = spread(solved, ("row", "col"), section)
        product = jnp.einsum(
            "jrc,cs->jrs",
            panels[section],
            solved,
            precision=lax.Precision.HIGHEST,
            preferred_element_type=jnp.float32,
        )
        remaining = jnp.where(
            block_owner > section,
            remaining - product,
            jnp.where(block_owner == section, solved[None], remaining),
        )
    return remaining


def solution(mesh):
    in_specs = (P(("row", "col"), None), P(None, None, ("row", "col"), None), P())
    out_specs = P(None, ("row", "col"), None)
    return jax.shard_map(
        per_device, mesh=mesh, in_specs=in_specs, out_specs=out_specs, check_vma=False
    )
```

profile of v0, /device:TPU:1, one launch (start us, length us, event | category | flops | bytes accessed | tf_op | source)
XLA Modules:
  0.0 1303.0 jit_solution(7980638426046954538)
XLA Ops:
  6.5 2.5 copy.19
  9.0 3.7 copy.12
  12.7 11.5 all-to-all-start
  24.2 0.0 all-reduce.9.cloned.1.call-start
  24.3 41.0 %all-to-all-done = f32[4,6,128,256]{3,0,1,2:T(4,128)S(1)} async-done(((f32[4,6,128,256]{3,0,1,2:T(4,128)}), f32[4,6,128,256]{3,0,1,2:T(4,128)S(1)}, u32[]{:S(2)}, u32[]{:S(2)}) %all-to-all-start) | async-done | bytes 3145760 | tf_op jit(solution)/shard_map/all_to_all | solution.py:17
  65.3 2.2 copy.13
  67.5 3.2 reshape.70
  70.7 0.0 copy-start.3
  70.7 2.6 convolution_select_fusion.7
  73.2 0.0 all-reduce.9.cloned.1.call-update
  73.3 0.5 all-reduce.11.cloned.1.call-start
  73.8 141.1 %all-reduce.9.cloned.1.call-done = f32[256,512]{1,0:T(8,128)} async-done(((f32[256,512]{1,0:T(8,128)}), f32[256,512]{1,0:T(8,128)}) %all-reduce.9.cloned.1.call-update) | async-done | bytes 524304 | tf_op jit(solution)/shard_map/psum | solution.py:9
  214.9 2.0 copy.15
  216.9 0.0 copy-done.3
  216.9 8.6 fusion.7
  225.6 2.4 fusion.30
  227.9 0.0 all-reduce.11.cloned.1.call-update
  227.9 0.0 all-reduce.13.cloned.1.call-start
  228.0 143.9 %all-reduce.11.cloned.1.call-done = f32[256,512]{0,1:T(8,128)} async-done(((f32[256,512]{0,1:T(8,128)}), f32[256,512]{0,1:T(8,128)}) %all-reduce.11.cloned.1.call-update) | async-done | bytes 524304 | tf_op jit(solution)/shard_map/psum | solution.py:9
  371.9 4.8 fusion.6
  376.7 0.0 copy-start
  376.7 1.7 copy-done
  378.4 2.4 fusion.29
  380.7 0.0 all-reduce.13.cloned.1.call-update
  380.8 0.2 all-reduce.15.cloned.1.call-start
  381.0 143.7 %all-reduce.13.cloned.1.call-done = f32[256,512]{0,1:T(8,128)} async-done(((f32[256,512]{0,1:T(8,128)}), f32[256,512]{0,1:T(8,128)}) %all-reduce.13.cloned.1.call-update) | async-done | bytes 524304 | tf_op jit(solution)/shard_map/psum | solution.py:9
  524.7 5.5 fusion.5
  530.3 2.4 fusion.28
  532.7 0.0 all-reduce.15.cloned.1.call-update
  532.7 0.0 all-reduce.17.cloned.1.call-start
  532.8 143.9 %all-reduce.15.cloned.1.call-done = f32[256,512]{0,1:T(8,128)} async-done(((f32[256,512]{0,1:T(8,128)}), f32[256,512]{0,1:T(8,128)}) %all-reduce.15.cloned.1.call-update) | async-done | bytes 524304 | tf_op jit(solution)/shard_map/psum | solution.py:9
  676.7 4.8 fusion.4
  681.4 0.0 copy-start.1
  681.5 1.7 copy-done.1
  683.1 2.4 fusion.27
  685.5 0.0 all-reduce.17.cloned.1.call-update
  685.5 0.0 all-reduce.19.cloned.1.call-start
  685.6 143.9 %all-reduce.17.cloned.1.call-done = f32[256,512]{0,1:T(8,128)} async-done(((f32[256,512]{0,1:T(8,128)}), f32[256,512]{0,1:T(8,128)}) %all-reduce.17.cloned.1.call-update) | async-done | bytes 524304 | tf_op jit(solution)/shard_map/psum | solution.py:9
  829.5 5.5 fusion.3
  835.0 2.4 fusion.26
  837.4 0.0 all-reduce.19.cloned.1.call-update
  837.4 0.3 all-reduce.21.cloned.1.call-start
  837.7 143.8 %all-reduce.19.cloned.1.call-done = f32[256,512]{0,1:T(8,128)} async-done(((f32[256,512]{0,1:T(8,128)}), f32[256,512]{0,1:T(8,128)}) %all-reduce.19.cloned.1.call-update) | async-done | bytes 524304 | tf_op jit(solution)/shard_map/psum | solution.py:9
  981.5 4.8 fusion.2
  986.2 0.0 copy-start.2
  986.3 1.7 copy-done.2
  987.9 2.4 fusion.25
  990.3 0.0 all-reduce.21.cloned.1.call-update
  990.3 0.0 all-reduce.23.cloned.1.call-start
  990.4 143.9 %all-reduce.21.cloned.1.call-done = f32[256,512]{0,1:T(8,128)} async-done(((f32[256,512]{0,1:T(8,128)}), f32[256,512]{0,1:T(8,128)}) %all-reduce.21.cloned.1.call-update) | async-done | bytes 524304 | tf_op jit(solution)/shard_map/psum | solution.py:9
  1134.3 5.5 fusion.1
  1139.8 2.4 fusion.24
  1142.2 0.0 all-reduce.23.cloned.1.call-update
  1142.2 143.9 %all-reduce.23.cloned.1.call-done = f32[256,512]{0,1:T(8,128)} async-done(((f32[256,512]{0,1:T(8,128)}), f32[256,512]{0,1:T(8,128)}) %all-reduce.23.cloned.1.call-update) | async-done | bytes 524304 | tf_op jit(solution)/shard_map/psum | solution.py:9
  1286.2 6.3 fusion
  1292.4 3.5 copy.16
  (8 shorter events, 0.1 us)
Async XLA Ops:
  12.7 52.5 %all-to-all-start = ((f32[4,6,128,256]{3,0,1,2:T(4,128)}), f32[4,6,128,256]{3,0,1,2:T(4,128)S(1)}, u32[]{:S(2)}, u32[]{:S(2)}) async-start(f32[4,6,128,256]{3,0,1,2:T(4,128)} %copy.12), calls=%async_computation | async-start | bytes 6291456 | tf_op jit(solution)/shard_map/all_to_all | solution.py:17
  24.2 190.7 %all-reduce.9.cloned.1.call-start = ((), (), s32[]{:S(2)}) async-start(), calls=%async_computation.1 | async-start | bytes 1048576 | tf_op jit(solution)/shard_map/psum | solution.py:9
  70.7 146.3 %copy-start.3 = (f32[512,6,256]{2,0,1:T(8,128)}, f32[512,6,256]{2,0,1:T(8,128)S(1)}, u32[]{:S(2)}) copy-start(f32[512,6,256]{2,0,1:T(8,128)S(1)} %reshape.70) | copy-start | bytes 9437188
  73.3 298.6 %all-reduce.11.cloned.1.call-start = ((), (), s32[]{:S(2)}) async-start(), calls=%async_computation.2 | async-start | bytes 1048576 | tf_op jit(solution)/shard_map/psum | solution.py:9
  227.9 296.8 %all-reduce.13.cloned.1.call-start = ((), (), s32[]{:S(2)}) async-start(), calls=%async_computation.3 | async-start | bytes 1048576 | tf_op jit(solution)/shard_map/psum | solution.py:9
  376.7 1.7 copy-start
  380.8 295.9 %all-reduce.15.cloned.1.call-start = ((), (), s32[]{:S(2)}) async-start(), calls=%async_computation.4 | async-start | bytes 1048576 | tf_op jit(solution)/shard_map/psum | solution.py:9
  532.7 296.8 %all-reduce.17.cloned.1.call-start = ((), (), s32[]{:S(2)}) async-start(), calls=%async_computation.5 | async-start | bytes 1048576 | tf_op jit(solution)/shard_map/psum | solution.py:9
  681.4 1.7 copy-start.1
  685.5 296.0 %all-reduce.19.cloned.1.call-start = ((), (), s32[]{:S(2)}) async-start(), calls=%async_computation.6 | async-start | bytes 1048576 | tf_op jit(solution)/shard_map/psum | solution.py:9
  837.4 296.8 %all-reduce.21.cloned.1.call-start = ((), (), s32[]{:S(2)}) async-start(), calls=%async_computation.7 | async-start | bytes 1048576 | tf_op jit(solution)/shard_map/psum | solution.py:9
  986.2 1.7 copy-start.2
  990.3 295.9 %all-reduce.23.cloned.1.call-start = ((), (), s32[]{:S(2)}) async-start(), calls=%async_computation.8 | async-start | bytes 1048576 | tf_op jit(solution)/shard_map/psum | solution.py:9
Sparse Core Ops, SparseCore 0:
  73.4 141.4 all-reduce.8
  228.1 143.8 all-reduce.10
  380.9 143.8 all-reduce.12
  532.8 143.8 all-reduce.14
  685.6 143.8 all-reduce.16
  837.6 143.8 all-reduce.18
  990.4 143.7 all-reduce.20
  1142.3 143.7 all-reduce.22
where the time goes:
time: 1310 us; the launch traced here: 1300 us
  waiting for transfers between devices  1190 us (91%)
  matrix products  65 us (5%)
  local copies, waits for them, and re-layouts  22.1 us (2%)
  between operations  13.9 us (1%)
    psum x8, waiting for transfers between devices, spread(): return lax.psum(block, axis)  1150 us
    dot_general x8, matrix products, per_device(): jnp.einsum('jrc,cs->jrs', panels[section], solved, precision=lax.Precisio...  45.8 us
    all_to_all x1, waiting for transfers between devices, per_device(): lax.all_to_all(pieces, ('row', 'col'), split_axis=2, concat_axis=0, tiled...  41 us
  transfers between devices with their start and end apart: 9, of which 9 were waited for; matrix products, arithmetic and copies ran while one was open for 0% of the time, Pallas kernels for 0%

commit v1 on v0

--- a/solution.py
+++ b/solution.py
@@ -14,7 +14,15 @@
     sections, blocks, width_block, _ = panels.shape
     devices = lax.axis_size(("row", "col"))
     pieces = snapshots.reshape(local_count, blocks, devices, width_block)
-    arrived = lax.all_to_all(pieces, ("row", "col"), split_axis=2, concat_axis=0, tiled=True)
+    arrived = jnp.concatenate(
+        lax.all_to_all(
+            jnp.stack(jnp.split(pieces, lax.axis_size(("row", "col")), axis=2)),
+            ("row", "col"),
+            0,
+            0,
+        ),
+        axis=0,
+    )
     remaining = jnp.transpose(
         arrived.reshape(devices * local_count, blocks, width_block), (1, 2, 0)
     )

time: 1310 us -> 1310 us (level)
  no operation moved by 1% of the time
where the time goes in v1:
time: 1310 us; the launch traced here: 1300 us
  waiting for transfers between devices  1190 us (91%)
  matrix products  62 us (5%)
  local copies, waits for them, and re-layouts  22.9 us (2%)
  between operations  14.3 us (1%)
    psum x8, waiting for transfers between devices, spread(): return lax.psum(block, axis)  1150 us
    dot_general x8, matrix products, per_device(): jnp.einsum('jrc,cs->jrs', panels[section], solved, precision=lax.Precisio...  42.8 us
    all_to_all x1, waiting for transfers between devices, per_device(): lax.all_to_all(jnp.stack(jnp.split(pieces, lax.axis_size(('row', 'col')),...  41 us
  transfers between devices with their start and end apart: 9, of which 9 were waited for; matrix products, arithmetic and copies ran while one was open for 0% of the time, Pallas kernels for 0%

profile of v1, /device:TPU:1, one launch (start us, length us, event | category | flops | bytes accessed | tf_op | source)
XLA Modules:
  0.0 1301.2 jit_solution(635419692808135040)
XLA Ops:
  6.5 2.5 copy.138
  13.5 2.5 copy.135
  15.9 11.5 all-to-all-start
  27.4 0.0 all-reduce.9.cloned.1.call-start
  27.5 41.0 %all-to-all-done = f32[128,4,6,1,256]{4,1,2,3,0:T(4,128)S(1)} async-done(((f32[128,4,6,1,256]{4,1,2,3,0:T(4,128)}), f32[128,4,6,1,256]{4,1,2,3,0:T(4,128)S(1)}, u32[]{:S(2)}, u32[]{:S(2)}) %all-to-all-start) | async-done | bytes 3145760 | tf_op jit(solution)/shard_map/all_to_all | solution.py:18
  68.5 2.2 copy.136
  70.7 3.2 reshape_reshape.3
  73.9 0.0 copy-start.3
  73.9 2.6 fusion.31
  76.5 0.0 all-reduce.9.cloned.1.call-update
  76.5 0.0 all-reduce.11.cloned.1.call-start
  76.5 141.5 %all-reduce.9.cloned.1.call-done = f32[256,512]{0,1:T(8,128)} async-done(((f32[256,512]{0,1:T(8,128)}), f32[256,512]{0,1:T(8,128)}) %all-reduce.9.cloned.1.call-update) | async-done | bytes 524304 | tf_op jit(solution)/shard_map/psum | solution.py:9
  218.1 0.0 copy-done.3
  218.1 5.6 fusion.7
  223.7 2.4 fusion.30
  226.1 0.0 all-reduce.11.cloned.1.call-update
  226.1 0.5 all-reduce.13.cloned.1.call-start
  226.7 143.4 %all-reduce.11.cloned.1.call-done = f32[256,512]{0,1:T(8,128)} async-done(((f32[256,512]{0,1:T(8,128)}), f32[256,512]{0,1:T(8,128)}) %all-reduce.11.cloned.1.call-update) | async-done | bytes 524304 | tf_op jit(solution)/shard_map/psum | solution.py:9
  370.1 4.8 fusion.6
  374.9 0.0 copy-start
  374.9 1.7 copy-done
  376.5 2.4 fusion.29
  378.9 0.0 all-reduce.13.cloned.1.call-update
  378.9 0.0 all-reduce.15.cloned.1.call-start
  379.0 143.9 %all-reduce.13.cloned.1.call-done = f32[256,512]{0,1:T(8,128)} async-done(((f32[256,512]{0,1:T(8,128)}), f32[256,512]{0,1:T(8,128)}) %all-reduce.13.cloned.1.call-update) | async-done | bytes 524304 | tf_op jit(solution)/shard_map/psum | solution.py:9
  522.9 5.5 fusion.5
  528.5 2.4 fusion.28
  530.8 0.0 all-reduce.15.cloned.1.call-update
  530.8 0.0 all-reduce.17.cloned.1.call-start
  530.9 143.9 %all-reduce.15.cloned.1.call-done = f32[256,512]{0,1:T(8,128)} async-done(((f32[256,512]{0,1:T(8,128)}), f32[256,512]{0,1:T(8,128)}) %all-reduce.15.cloned.1.call-update) | async-done | bytes 524304 | tf_op jit(solution)/shard_map/psum | solution.py:9
  674.8 4.8 fusion.4
  679.6 0.0 copy-start.1
  679.6 1.7 copy-done.1
  681.2 2.4 fusion.27
  683.6 0.0 all-reduce.17.cloned.1.call-update
  683.6 0.2 all-reduce.19.cloned.1.call-start
  683.9 143.7 %all-reduce.17.cloned.1.call-done = f32[256,512]{0,1:T(8,128)} async-done(((f32[256,512]{0,1:T(8,128)}), f32[256,512]{0,1:T(8,128)}) %all-reduce.17.cloned.1.call-update) | async-done | bytes 524304 | tf_op jit(solution)/shard_map/psum | solution.py:9
  827.6 5.5 fusion.3
  833.2 2.4 fusion.26
  835.5 0.0 all-reduce.19.cloned.1.call-update
  835.6 0.0 all-reduce.21.cloned.1.call-start
  835.6 143.9 %all-reduce.19.cloned.1.call-done = f32[256,512]{0,1:T(8,128)} async-done(((f32[256,512]{0,1:T(8,128)}), f32[256,512]{0,1:T(8,128)}) %all-reduce.19.cloned.1.call-update) | async-done | bytes 524304 | tf_op jit(solution)/shard_map/psum | solution.py:9
  979.5 4.8 fusion.2
  984.3 0.0 copy-start.2
  984.3 1.7 copy-done.2
  986.0 2.4 fusion.25
  988.4 0.0 all-reduce.21.cloned.1.call-update
  988.4 0.3 all-reduce.23.cloned.1.call-start
  988.7 143.7 %all-reduce.21.cloned.1.call-done = f32[256,512]{0,1:T(8,128)} async-done(((f32[256,512]{0,1:T(8,128)}), f32[256,512]{0,1:T(8,128)}) %all-reduce.21.cloned.1.call-update) | async-done | bytes 524304 | tf_op jit(solution)/shard_map/psum | solution.py:9
  1132.4 5.5 fusion.1
  1137.9 2.4 fusion.24
  1140.3 0.0 all-reduce.23.cloned.1.call-update
  1140.3 144.0 %all-reduce.23.cloned.1.call-done = f32[256,512]{0,1:T(8,128)} async-done(((f32[256,512]{0,1:T(8,128)}), f32[256,512]{0,1:T(8,128)}) %all-reduce.23.cloned.1.call-update) | async-done | bytes 524304 | tf_op jit(solution)/shard_map/psum | solution.py:9
  1284.3 6.2 fusion
  1290.6 3.5 copy.137
  (136 shorter events, 4.1 us)
Async XLA Ops:
  15.9 52.5 %all-to-all-start = ((f32[128,4,6,1,256]{4,1,2,3,0:T(4,128)}), f32[128,4,6,1,256]{4,1,2,3,0:T(4,128)S(1)}, u32[]{:S(2)}, u32[]{:S(2)}) async-start(f32[128,4,6,1,256]{4,1,2,3,0:T(4,128)} %copy.135), calls=%async_computation | async-start | bytes 6291456 | tf_op jit(solution)/shard_map/all_to_all | solution.py:18
  27.4 190.6 %all-reduce.9.cloned.1.call-start = ((), (), s32[]{:S(2)}) async-start(), calls=%async_computation.1 | async-start | bytes 1048576 | tf_op jit(solution)/shard_map/psum | solution.py:9
  73.9 144.2 %copy-start.3 = (f32[512,6,256]{2,0,1:T(8,128)}, f32[512,6,256]{2,0,1:T(8,128)S(1)}, u32[]{:S(2)}) copy-start(f32[512,6,256]{2,0,1:T(8,128)S(1)} %reshape_reshape.3) | copy-start | bytes 9437188
  76.5 293.6 %all-reduce.11.cloned.1.call-start = ((), (), s32[]{:S(2)}) async-start(), calls=%async_computation.2 | async-start | bytes 1048576 | tf_op jit(solution)/shard_map/psum | solution.py:9
  226.1 296.8 %all-reduce.13.cloned.1.call-start = ((), (), s32[]{:S(2)}) async-start(), calls=%async_computation.3 | async-start | bytes 1048576 | tf_op jit(solution)/shard_map/psum | solution.py:9
  374.9 1.7 copy-start
  378.9 295.9 %all-reduce.15.cloned.1.call-start = ((), (), s32[]{:S(2)}) async-start(), calls=%async_computation.4 | async-start | bytes 1048576 | tf_op jit(solution)/shard_map/psum | solution.py:9
  530.8 296.8 %all-reduce.17.cloned.1.call-start = ((), (), s32[]{:S(2)}) async-start(), calls=%async_computation.5 | async-start | bytes 1048576 | tf_op jit(solution)/shard_map/psum | solution.py:9
  679.6 1.7 copy-start.1
  683.6 295.9 %all-reduce.19.cloned.1.call-start = ((), (), s32[]{:S(2)}) async-start(), calls=%async_computation.6 | async-start | bytes 1048576 | tf_op jit(solution)/shard_map/psum | solution.py:9
  835.6 296.8 %all-reduce.21.cloned.1.call-start = ((), (), s32[]{:S(2)}) async-start(), calls=%async_computation.7 | async-start | bytes 1048576 | tf_op jit(solution)/shard_map/psum | solution.py:9
  984.3 1.7 copy-start.2
  988.4 296.0 %all-reduce.23.cloned.1.call-start = ((), (), s32[]{:S(2)}) async-start(), calls=%async_computation.8 | async-start | bytes 1048576 | tf_op jit(solution)/shard_map/psum | solution.py:9
Sparse Core Ops, SparseCore 0:
  76.6 141.4 all-reduce.8
  226.2 143.7 all-reduce.10
  379.0 143.8 all-reduce.12
  531.0 143.7 all-reduce.14
  683.8 143.8 all-reduce.16
  835.7 143.8 all-reduce.18
  988.5 143.8 all-reduce.20
  1140.4 143.8 all-reduce.22
